TPU v7x, 32 devices: a whole 2x2x4 slice. The times are simulated.
32 devices in a mesh: ctx: 8 (over z, core), fsdp: 4 (over y, x).
Axes of the slice: x: 2, y: 2, z: 4, core: 2. Of those that a mesh axis runs over, the one named last changes fastest.
Arguments:
- layer_in: bfloat16 [4, 8, 2, 128, 1024], P(None, 'ctx', None, 'fsdp'), may hold values from -6 to 6
- out_grad: bfloat16 [4, 8, 2, 128, 1024], P(None, 'ctx', None, 'fsdp'), may hold values from -6 to 6
- block_pairs: int32 [4, 8], replicated, may hold values from 0 to 7, each once within a row
- attn_gain: bfloat16 [1024], P('fsdp'), may hold values from 0.099609375 to 1.8984375
- attn_shift: bfloat16 [1024], P('fsdp'), may hold values from -3 to 3
- qkv_weight: bfloat16 [1024, 3072], P('fsdp'), may hold values from -0.25 to 0.25
- query_bias: bfloat16 [1024], P('fsdp'), may hold values from -3 to 3
- value_bias: bfloat16 [1024], P('fsdp'), may hold values from -0.29882812 to 0.29882812
- out_weight: bfloat16 [1024, 1024], P('fsdp'), may hold values from -2 to 2
- out_bias: bfloat16 [1024], P('fsdp'), may hold values from -3 to 3
- mlp_gain: bfloat16 [1024], P('fsdp'), may hold values from 0.099609375 to 1.8984375
- mlp_shift: bfloat16 [1024], P('fsdp'), may hold values from -3 to 3
- fc_weight: bfloat16 [1024, 4096], P('fsdp'), may hold values from -0.1875 to 0.1875
- fc_bias: bfloat16 [4096], P('fsdp'), may hold values from -3 to 3
- proj_weight: bfloat16 [4096, 1024], P('fsdp'), may hold values from -0.09375 to 0.09375
- proj_bias: bfloat16 [1024], P('fsdp'), may hold values from -3 to 3
Outputs:
- layer_out: bfloat16 [4, 8, 2, 128, 1024], P(None, 'ctx', None, 'fsdp')
- in_grad: float32 [4, 8, 2, 128, 1024], P(None, 'ctx', None, 'fsdp')
- attn_gain_grad: float32 [1024], P('fsdp')
- attn_shift_grad: float32 [1024], P('fsdp')
- qkv_weight_grad: float32 [1024, 3072], P('fsdp')
- query_bias_grad: float32 [1024], P('fsdp')
- value_bias_grad: float32 [1024], P('fsdp')
- out_weight_grad: float32 [1024, 1024], P('fsdp')
- out_bias_grad: float32 [1024], P('fsdp')
- mlp_gain_grad: float32 [1024], P('fsdp')
- mlp_shift_grad: float32 [1024], P('fsdp')
- fc_weight_grad: float32 [1024, 4096], P('fsdp')
- fc_bias_grad: float32 [4096], P('fsdp')
- proj_weight_grad: float32 [4096, 1024], P('fsdp')
- proj_bias_grad: float32 [1024], P('fsdp')
Inputs may be any that keep to these rules, and one draw needn't show every extreme that they name: `block_pairs`: each row is a permutation: every device of ctx holds exactly one block pair of every sequence.
All inputs are finite; a program needn't handle non-finite values.
Results may differ from a plain program's by a relative error of at most 0.023.
Values may be sent and summed in bfloat16 or wider, within the bound.
No kernel may reach another device: no remote copies, remote signals or barrier semaphores. Data moves between devices by JAX's collectives and lax.ppermute only.
A program may use at most 320 MiB of HBM per device.

v0:
```python
import jax
import jax.numpy as jnp
from jax import lax
from jax.sharding import PartitionSpec as P

HD = 64
norm_eps = 1e-05
masked_score = -1e30


def for_sending(array):
    return jax.tree.map(lambda a: a.astype(jnp.bfloat16) if a.dtype == jnp.float32 else a, array)


def layer_norm(values, gain, shift):
    average = jnp.mean(values, axis=-1, keepdims=True)
    centred = values - average
    spread = jnp.mean(centred * centred, axis=-1, keepdims=True)
    return centred * lax.rsqrt(spread + norm_eps) * gain + shift


def gelu_tanh(values):
    return jax.nn.gelu(values, approximate=True)


def contract_last(left, right):
    return lax.dot_general(
        left, right, (((1,), (1,)), ((), ())), preferred_element_type=jnp.float32
    )


def contract_first(left, right):
    return lax.dot_general(
        left, right, (((0,), (0,)), ((), ())), preferred_element_type=jnp.float32
    )


def head_scores(query, keys, query_places, key_places):
    scores = contract_last(query, keys)
    return jnp.where(key_places[None, :] <= query_places[:, None], scores, masked_score)


def score_grads(query, keys, values, grad_out, summary, row_sum, query_places, key_places):
    scores = head_scores(query, keys, query_places, key_places)
    probs = jnp.exp(scores - summary[:, None])
    grad_probs = contract_last(grad_out, values)
    row_sum = jnp.sum(probs * grad_probs, axis=1)
    grad_scores = (probs * (grad_probs - row_sum[:, None])).astype(jnp.bfloat16)
    return (probs.astype(jnp.bfloat16), grad_scores, row_sum)


def attend_forward(items):
    query, keys, values, query_places, key_places = items
    outputs = []
    summaries = []
    for head_index in range(query.shape[1] // HD):
        columns = slice(head_index * HD, (head_index + 1) * HD)
        scores = head_scores(query[:, columns], keys[:, columns], query_places, key_places)
        row_peak = jnp.max(scores, axis=1, keepdims=True)
        raised = jnp.exp(scores - row_peak)
        row_total = jnp.sum(raised, axis=1, keepdims=True)
        weights = (raised / row_total).astype(jnp.bfloat16)
        outputs.append(
            jnp.dot(weights, values[:, columns], preferred_element_type=jnp.float32).astype(
                jnp.bfloat16
            )
        )
        summaries.append(row_peak[:, 0] + jnp.log(row_total[:, 0]))
    return (jnp.concatenate(outputs, axis=1), jnp.stack(summaries, axis=1))


def attend_backward(items):
    query, keys, values, grad_out, summary, query_places, key_places = items
    query_parts, key_parts, value_parts = ([], [], [])
    for head_index in range(query.shape[1] // HD):
        columns = slice(head_index * HD, (head_index + 1) * HD)
        probs_low, grad_scores, row_sum = score_grads(
            query[:, columns],
            keys[:, columns],
            values[:, columns],
            grad_out[:, columns],
            summary[:, head_index],
            None,
            query_places,
            key_places,
        )
        query_parts.append(
            jnp.dot(grad_scores, keys[:, columns], preferred_element_type=jnp.float32).astype(
                jnp.bfloat16
            )
        )
        key_parts.append(contract_first(grad_scores, query[:, columns]))
        value_parts.append(contract_first(probs_low, grad_out[:, columns]))
    return (
        jnp.concatenate(query_parts, axis=1),
        jnp.concatenate(key_parts, axis=1),
        jnp.concatenate(value_parts, axis=1),
    )


CTX = ("zc", "core")


def gather_weight(shard):
    half = shard.shape[0] // 2
    piece = lax.dynamic_slice_in_dim(shard, lax.axis_index("core") * half, half, 0)
    fsdp_size = lax.axis_size("fsdp")
    pieces = lax.all_to_all(
        jnp.broadcast_to(piece[None], (fsdp_size,) + piece.shape),
        "fsdp",
        split_axis=0,
        concat_axis=0,
        tiled=True,
    )
    whole = lax.all_gather(pieces, "core", axis=1, tiled=True)
    return whole.reshape(-1, shard.shape[1])


def core_major(rows, fsdp_size):
    count, width = rows.shape
    return (
        rows.reshape(count, fsdp_size, 2, width // (2 * fsdp_size))
        .transpose(0, 2, 1, 3)
        .reshape(count, width)
    )


def reduce_weight_grad(grad):
    grad = lax.psum_scatter(grad.astype(jnp.bfloat16), "core", scatter_dimension=0, tiled=True)
    fsdp_size = lax.axis_size("fsdp")
    blocks = lax.all_to_all(
        grad.reshape((fsdp_size, -1) + grad.shape[1:]),
        "fsdp",
        split_axis=0,
        concat_axis=0,
        tiled=True,
    )
    grad = jnp.sum(blocks.astype(jnp.float32), axis=0).astype(jnp.bfloat16)
    grad = lax.psum_scatter(grad, "zc", scatter_dimension=0, tiled=True)
    grad = lax.all_gather(grad, "zc", axis=0, tiled=True)
    grad = lax.all_gather(grad, "core", axis=0, tiled=True)
    return grad.astype(jnp.float32)


def shards(
    layer_in,
    out_grad,
    block_pairs,
    attn_gain,
    attn_shift,
    qkv_weight,
    query_bias,
    value_bias,
    out_weight,
    out_bias,
    mlp_gain,
    mlp_shift,
    fc_weight,
    fc_bias,
    proj_weight,
    proj_bias,
):
    fsdp_size = lax.axis_size("fsdp")
    ctx_size = lax.axis_size("zc") * lax.axis_size("core")
    seq_count = layer_in.shape[0]
    half_rows = layer_in.shape[3]
    model_width = layer_in.shape[4]
    block_len = half_rows * fsdp_size
    pair_len = 2 * block_len
    group_width = model_width // fsdp_size
    gathered = (
        gather_weight(qkv_weight),
        gather_weight(out_weight),
        gather_weight(fc_weight),
        gather_weight(proj_weight),
    )
    qkv_full, out_full, fc_full, proj_full = (gathered[0], gathered[1], gathered[2], gathered[3])
    vector_shards = (
        attn_gain,
        attn_shift,
        query_bias,
        value_bias,
        out_bias,
        mlp_gain,
        mlp_shift,
        fc_bias,
        proj_bias,
    )
    vector_pieces = lax.all_gather(jnp.concatenate(vector_shards), "fsdp", axis=0, tiled=False)
    vectors = []
    start = 0
    for shard in vector_shards:
        vectors.append(
            vector_pieces[:, start : start + shard.shape[0]].reshape(-1).astype(jnp.float32)
        )
        start += shard.shape[0]
    (
        gain_attn,
        shift_attn,
        bias_query,
        bias_value,
        bias_out,
        gain_mlp,
        shift_mlp,
        bias_fc,
        bias_proj,
    ) = vectors
    halves = jnp.stack([block_pairs, 2 * ctx_size - 1 - block_pairs], axis=2)
    key_places = (halves[..., None] * block_len + jnp.arange(block_len, dtype=jnp.int32)).reshape(
        seq_count, ctx_size, pair_len
    )
    query_places = lax.dynamic_slice_in_dim(key_places, lax.axis_index(CTX), 1, 1).reshape(
        seq_count, pair_len
    )
    key_places = key_places.reshape(seq_count, ctx_size * pair_len)
    inputs = layer_in.reshape(-1, model_width).astype(jnp.float32)
    normed, attn_norm_back = jax.vjp(layer_norm, inputs, gain_attn, shift_attn)
    normed_low = normed.astype(jnp.bfloat16)
    mixed = jnp.dot(normed_low, qkv_full, preferred_element_type=jnp.float32)
    query = ((mixed[:, :model_width] + bias_query) * 0.125).astype(jnp.bfloat16)
    keys = mixed[:, model_width : 2 * model_width].astype(jnp.bfloat16)
    values = (mixed[:, 2 * model_width :] + bias_value).astype(jnp.bfloat16)

    def to_groups(array):
        return array.reshape(seq_count, 2, half_rows, fsdp_size, group_width)

    def to_pairs(array):
        return array.reshape(seq_count, 2, block_len, 1, group_width)

    qkv_heads = lax.all_to_all(
        jnp.concatenate([to_groups(query), to_groups(keys), to_groups(values)], axis=4),
        "fsdp",
        split_axis=3,
        concat_axis=2,
        tiled=True,
    ).reshape(seq_count, pair_len, 3 * group_width)
    query_heads = qkv_heads[..., :group_width]
    own_kv = qkv_heads[..., group_width:]
    kv_all = lax.all_gather(
        own_kv.reshape(seq_count, 1, pair_len, 2 * group_width), CTX, axis=1, tiled=True
    )
    key_all = kv_all[..., :group_width]
    value_all = kv_all[..., group_width:]
    key_all = key_all.reshape(seq_count, -1, group_width)
    value_all = value_all.reshape(seq_count, -1, group_width)
    attended, summary = lax.map(
        attend_forward, (query_heads, key_all, value_all, query_places, key_places)
    )
    attended_rows = lax.all_to_all(
        for_sending(to_pairs(attended)), "fsdp", split_axis=2, concat_axis=3, tiled=True
    ).reshape(-1, model_width)
    branch = jnp.dot(attended_rows, out_full, preferred_element_type=jnp.float32) + bias_out
    middle = inputs + branch
    normed_mlp, mlp_norm_back = jax.vjp(layer_norm, middle, gain_mlp, shift_mlp)
    mlp_low = normed_mlp.astype(jnp.bfloat16)
    hidden = jnp.dot(mlp_low, fc_full, preferred_element_type=jnp.float32) + bias_fc
    activated, gelu_back = jax.vjp(gelu_tanh, hidden)
    activated_low = activated.astype(jnp.bfloat16)
    result = (
        middle + jnp.dot(activated_low, proj_full, preferred_element_type=jnp.float32) + bias_proj
    )
    layer_out = result.astype(jnp.bfloat16).reshape(layer_in.shape)
    grad_rows = out_grad.reshape(-1, model_width)
    grad_result = grad_rows.astype(jnp.float32)
    proj_grad = contract_first(core_major(activated_low, fsdp_size), grad_rows)
    proj_bias_grad = jnp.sum(grad_result, axis=0)
    grad_activated = contract_last(grad_rows, proj_full)
    grad_hidden = gelu_back(grad_activated)[0].astype(jnp.bfloat16)
    fc_grad = contract_first(core_major(mlp_low, fsdp_size), grad_hidden)
    fc_bias_grad = jnp.sum(grad_hidden.astype(jnp.float32), axis=0)
    grad_middle, mlp_gain_grad, mlp_shift_grad = mlp_norm_back(contract_last(grad_hidden, fc_full))
    grad_middle = grad_middle + grad_result
    grad_branch = grad_middle.astype(jnp.bfloat16)
    out_weight_term = contract_first(core_major(attended_rows, fsdp_size), grad_branch)
    out_bias_grad = jnp.sum(grad_branch.astype(jnp.float32), axis=0)
    grad_attended = contract_last(grad_branch, out_full).astype(jnp.bfloat16)
    grad_heads = lax.all_to_all(
        to_groups(grad_attended), "fsdp", split_axis=3, concat_axis=2, tiled=True
    ).reshape(seq_count, pair_len, group_width)
    grad_query, grad_keys, grad_values = lax.map(
        attend_backward,
        (query_heads, key_all, value_all, grad_heads, summary, query_places, key_places),
    )
    kv_grads = jnp.concatenate([grad_keys, grad_values], axis=2).astype(jnp.bfloat16)
    kv_grads = kv_grads.reshape(seq_count, ctx_size, pair_len, 2 * group_width).transpose(
        1, 0, 2, 3
    )
    kv_part = lax.psum_scatter(
        kv_grads.reshape(ctx_size * seq_count * pair_len, 2 * group_width),
        CTX,
        scatter_dimension=0,
        tiled=True,
    ).reshape(seq_count, pair_len, 2 * group_width)
    key_part = kv_part[..., :group_width].astype(jnp.float32)
    value_part = kv_part[..., group_width:].astype(jnp.float32)
    key_grad_low = key_part.astype(jnp.bfloat16)
    value_grad_low = value_part.astype(jnp.bfloat16)
    query_back, key_back, value_back = (
        lax.all_to_all(
            for_sending(to_pairs(grad_query)), "fsdp", split_axis=2, concat_axis=3, tiled=True
        ),
        lax.all_to_all(
            for_sending(to_pairs(key_grad_low)), "fsdp", split_axis=2, concat_axis=3, tiled=True
        ),
        lax.all_to_all(
            for_sending(to_pairs(value_grad_low)), "fsdp", split_axis=2, concat_axis=3, tiled=True
        ),
    )
    grad_mixed = jnp.concatenate(
        [
            query_back.reshape(-1, model_width) * 0.125,
            key_back.reshape(-1, model_width),
            value_back.reshape(-1, model_width),
        ],
        axis=1,
    )
    qkv_grad = contract_first(core_major(normed_low, fsdp_size), grad_mixed)
    mixed_float = grad_mixed.astype(jnp.float32)
    query_bias_grad = jnp.sum(mixed_float[:, :model_width], axis=0)
    value_bias_grad = jnp.sum(mixed_float[:, 2 * model_width :], axis=0)
    grad_inputs, attn_gain_grad, attn_shift_grad = attn_norm_back(
        contract_last(grad_mixed, qkv_full)
    )
    in_grad = (grad_inputs + grad_middle).reshape(layer_in.shape)
    weight_totals = tuple(
        (reduce_weight_grad(grad) for grad in (qkv_grad, out_weight_term, fc_grad, proj_grad))
    )
    vector_grads = (
        attn_gain_grad,
        attn_shift_grad,
        query_bias_grad,
        value_bias_grad,
        out_bias_grad,
        mlp_gain_grad,
        mlp_shift_grad,
        fc_bias_grad,
        proj_bias_grad,
    )
    packed = jnp.concatenate([grad.reshape(fsdp_size, -1) for grad in vector_grads], axis=1)
    packed = lax.psum(packed.astype(jnp.float32), CTX + ("fsdp",))
    packed = lax.dynamic_index_in_dim(packed, lax.axis_index("fsdp"), 0, keepdims=False)
    vector_totals = []
    offset = 0
    for grad in vector_grads:
        width = grad.shape[0] // fsdp_size
        vector_totals.append(packed[offset : offset + width])
        offset += width
    totals = weight_totals + tuple(vector_totals)
    return (
        layer_out,
        in_grad,
        totals[4],
        totals[5],
        totals[0],
        totals[6],
        totals[7],
        totals[1],
        totals[8],
        totals[9],
        totals[10],
        totals[2],
        totals[11],
        totals[3],
        totals[12],
    )


def solution(mesh):
    ctx_count, fsdp_count = mesh.devices.shape
    mesh = jax.sharding.Mesh(
        mesh.devices.reshape(ctx_count // 2, 2, fsdp_count), ("zc", "core", "fsdp")
    )
    placed = (
        P(None, CTX, None, "fsdp", None),
        P(None, CTX, None, "fsdp", None),
        P(),
        P("fsdp"),
        P("fsdp"),
        P("fsdp", None),
        P("fsdp"),
        P("fsdp"),
        P("fsdp", None),
        P("fsdp"),
        P("fsdp"),
        P("fsdp"),
        P("fsdp", None),
        P("fsdp"),
        P("fsdp", None),
        P("fsdp"),
    )
    return jax.shard_map(
        shards,
        mesh=mesh,
        in_specs=placed,
        out_specs=(
            P(None, CTX, None, "fsdp", None),
            P(None, CTX, None, "fsdp", None),
            P("fsdp"),
            P("fsdp"),
            P("fsdp", None),
            P("fsdp"),
            P("fsdp"),
            P("fsdp", None),
            P("fsdp"),
            P("fsdp"),
            P("fsdp"),
            P("fsdp", None),
            P("fsdp"),
            P("fsdp", None),
            P("fsdp"),
        ),
        check_vma=False,
    )
```

profile of v0, /device:TPU:0, one launch (start us, length us, event | category | flops | bytes accessed | tf_op | source)
XLA Modules:
  0.0 879.7 jit_solution(5103445620654060094)
XLA Ops:
  9.0 41.7 %all_to_all.124 = bf16[4,128,3072]{2,1,0:T(8,128)(2,1)} all-to-all(bf16[4,128,3072]{2,1,0:T(8,128)(2,1)S(1)} %broadcast_in_dim.65), channel_id=1, replica_groups=mesh['zc'=4,'core'=2,'fsdp'=4] {'fsdp'}, dimensions={0} | all-to-all | bytes 6291456 | tf_op jit(solution)/shard_map/all_to_all | solution.py:108
  53.2 7.6 all-gather
  62.8 4.6 all-gather.13.cloned.1.call-done
  67.4 4.6 fusion.102
  83.4 23.9 %all_to_all.125 = bf16[4,2,32,4,768]{4,2,1,0,3:T(8,128)(2,1)S(1)} all-to-all(bf16[4,2,32,4,768]{4,2,1,0,3:T(8,128)(2,1)S(1)} %pad_maximum_fusion), channel_id=1, replica_groups=mesh['zc'=4,'core'=2,'fsdp'=4] {'fsdp'}, dimensions={3} | all-to-all | bytes 3145728 | tf_op jit(solution)/shard_map/all_to_all | solution.py:230
  110.9 4.3 all-to-all-start.3
  116.2 11.9 %all-to-all-done.3 = bf16[4,128,1024]{2,1,0:T(8,128)(2,1)} async-done(((bf16[4,128,1024]{2,1,0:T(8,128)(2,1)}), bf16[4,128,1024]{2,1,0:T(8,128)(2,1)}, u32[]{:S(2)}, u32[]{:S(2)}) %all-to-all-start.3) | async-done | bytes 1048608 | tf_op jit(solution)/shard_map/all_to_all | solution.py:108
  128.1 3.7 broadcast_in_dim.67
  131.8 4.8 all-to-all-start.4
  137.4 46.1 %all-to-all-done.4 = bf16[4,128,4096]{2,1,0:T(8,128)(2,1)} async-done(((bf16[4,128,4096]{2,1,0:T(8,128)(2,1)}), bf16[4,128,4096]{2,1,0:T(8,128)(2,1)}, u32[]{:S(2)}, u32[]{:S(2)}) %all-to-all-start.4) | async-done | bytes 4194336 | tf_op jit(solution)/shard_map/all_to_all | solution.py:108
  187.9 5.0 all-to-all-start.5
  193.5 46.2 %all-to-all-done.5 = bf16[4,512,1024]{2,1,0:T(8,128)(2,1)} async-done(((bf16[4,512,1024]{2,1,0:T(8,128)(2,1)}), bf16[4,512,1024]{2,1,0:T(8,128)(2,1)}, u32[]{:S(2)}, u32[]{:S(2)}) %all-to-all-start.5) | async-done | bytes 4194336 | tf_op jit(solution)/shard_map/all_to_all | solution.py:108
  241.6 6.5 fusion.98
  248.2 41.8 %while.26 = (s32[]{:T(128)}, bf16[4,256,256]{2,1,0:T(8,128)(2,1)S(1)}, f32[4,256,4]{1,2,0:T(4,128)}, s32[4,2048]{1,0:T(4,128)S(1)}, s32[4,256]{1,0:T(4,128)S(1)}...) while((s32[]{:T(128)}, ...), condition=%wide.region_11.12_spmd, body=%wide.region_2.11_spmd.sunk | while | flops 554240000 | bytes 35092604 | solution.py:246
  291.3 3.7 all-to-all-start.2
  295.2 6.8 all-to-all-done.2
  306.8 9.5 %multiply_convert_fusion.4 = (bf16[256,4096]{1,0:T(8,128)(2,1)}, f32[256,4096]{1,0:T(8,128)}) fusion(f32[4096]{0:T(1024)S(1)} %bitcast.361, bf16[256,1024]{1,0:T(8,128)(2,1)S(1)} %add_convert_fusion.1, bf16[1024,4096]{1,0:T(8,128)(2,1)} %bitcast.375), kind=kOutput, calls=%fused_computation.142 | convolution fusion | flops 2157969408 | bytes 15220736 | tf_op jit(solution)/shard_map/dot_general | solution.py:256
  316.2 12.6 %convert_reduce_fusion = (f32[4096]{0:T(1024)}, bf16[256,4096]{1,0:T(8,128)(2,1)S(1)}) fusion(f32[256,4096]{1,0:T(8,128)} %get-tuple-element.305, bf16[4096,1024]{1,0:T(8,128)(2,1)} %bitcast.373, bf16[256,1024]{1,0:T(8,128)(2,1)S(1)} %bitcast.285), kind=kOutput, calls=%fused_computation.141 | convolution fusion | flops 2170548224 | bytes 15220736 | tf_op jit(solution)/shard_map/dot_general | solution.py:27
  341.2 7.2 convolution_convert_fusion.9
  349.3 118.0 %while.27 = (s32[]{:T(128)}, bf16[4,256,256]{2,1,0:T(8,128)(2,1)}, bf16[4,2048,256]{2,1,0:T(8,128)(2,1)}, bf16[4,2048,256]{2,1,0:T(8,128)(2,1)}, s32[4,2048]{1,0...) while((s32[]{:T(128)}, bf16[4,256,256]{2,1,0:T(8,128)(2,1)}, ...), condition=%wide.region_21.22_spmd, body=%wide.region_16.21_spmd.sunk | while | flops 1370029056 | bytes 166414960 | solution.py:280
  467.3 7.6 maximum_bitcast_fusion.5
  474.9 7.5 copy.115
  486.9 4.8 copy.126
  491.8 5.6 convolution_convert_fusion.8
  497.5 51.6 %all_to_all.127 = bf16[4,128,4096]{2,1,0:T(8,128)(2,1)} all-to-all(bf16[4,128,4096]{2,1,0:T(8,128)(2,1)} %bitcast.300), channel_id=1, replica_groups=mesh['zc'=4,'core'=2,'fsdp'=4] {'fsdp'}, dimensions={0} | all-to-all | bytes 8388608 | tf_op jit(solution)/shard_map/all_to_all | solution.py:131
  549.1 4.3 reduce_sum.324
  561.4 12.0 %reduce-scatter.10.cloned.1.call-done = bf16[1024,512]{1,0:T(8,128)(2,1)} async-done(((bf16[8192,512]{1,0:T(8,128)(2,1)}), bf16[1024,512]{1,0:T(8,128)(2,1)}) %reduce-scatter.10.cloned.1.call-update) | async-done | bytes 1048592 | tf_op jit(solution)/shard_map/reduce_scatter | solution.py:288
  576.0 3.6 all-to-all-start.8
  581.1 5.2 all-to-all-done.8
  586.3 4.2 all-to-all-start.9
  599.0 5.8 fusion.90
  607.9 4.5 convolution_convert_fusion.10
  612.5 49.4 %all_to_all.128 = bf16[4,512,1024]{2,1,0:T(8,128)(2,1)} all-to-all(bf16[4,512,1024]{2,1,0:T(8,128)(2,1)} %bitcast.301), channel_id=1, replica_groups=mesh['zc'=4,'core'=2,'fsdp'=4] {'fsdp'}, dimensions={0} | all-to-all | bytes 8388608 | tf_op jit(solution)/shard_map/all_to_all | solution.py:131
  662.0 4.4 reduce_sum.325
  667.2 13.4 %all_to_all.126 = bf16[4,128,1024]{2,1,0:T(8,128)(2,1)S(1)} all-to-all(bf16[4,128,1024]{2,1,0:T(8,128)(2,1)} %bitcast.329), channel_id=1, replica_groups=mesh['zc'=4,'core'=2,'fsdp'=4] {'fsdp'}, dimensions={0} | all-to-all | bytes 2097152 | tf_op jit(solution)/shard_map/all_to_all | solution.py:131
  680.6 4.7 all-to-all-start.10
  685.4 12.1 %reduce-scatter.26.cloned.1.call-done = bf16[128,1024]{1,0:T(8,128)(2,1)} async-done(((bf16[512,1024]{1,0:T(8,128)(2,1)}), bf16[128,1024]{1,0:T(8,128)(2,1)}) %reduce-scatter.26.cloned.1.call-update) | async-done | bytes 262160 | tf_op jit(solution)/shard_map/reduce_scatter | solution.py:139
  698.5 16.4 %all-to-all-done.10 = bf16[4,128,3072]{2,1,0:T(8,128)(2,1)} async-done(((bf16[4,128,3072]{2,1,0:T(8,128)(2,1)}), bf16[4,128,3072]{2,1,0:T(8,128)(2,1)}, u32[]{:S(2)}, u32[]{:S(2)}) %all-to-all-start.10) | async-done | bytes 3145760 | tf_op jit(solution)/shard_map/all_to_all | solution.py:131
  714.9 3.6 reduce_sum.322
  718.6 7.0 all-gather.23.cloned.1.call-done
  725.6 28.7 %all-gather.27.cloned.1.call-done = bf16[512,1024]{1,0:T(8,128)(2,1)} async-done(((bf16[128,1024]{1,0:T(8,128)(2,1)}), bf16[512,1024]{1,0:T(8,128)(2,1)}) %all-gather.27.cloned.1.call-update) | async-done | bytes 1048592 | tf_op jit(solution)/shard_map/all_gather | solution.py:140
  756.0 7.2 fusion.78
  763.2 12.7 %reduce-scatter.18.cloned.1.call-done = bf16[32,1024]{1,0:T(8,128)(2,1)} async-done(((bf16[128,1024]{1,0:T(8,128)(2,1)}), bf16[32,1024]{1,0:T(8,128)(2,1)}) %reduce-scatter.18.cloned.1.call-update) | async-done | bytes 65552 | tf_op jit(solution)/shard_map/reduce_scatter | solution.py:139
  775.9 15.6 %all_gather.54 = bf16[128,1024]{1,0:T(8,128)(2,1)S(1)} all-gather(bf16[32,1024]{1,0:T(8,128)(2,1)} %reduce-scatter.18.cloned.1.call-done), channel_id=1, replica_groups=mesh['zc'=4,'core'=2,'fsdp'=4] {'zc'}, dimensions={0}, use_global_device_ids=true | all-gather | bytes 327680 | tf_op jit(solution)/shard_map/all_gather | solution.py:140
  800.7 18.2 %all_gather.52 = bf16[128,3072]{1,0:T(8,128)(2,1)} all-gather(bf16[32,3072]{1,0:T(8,128)(2,1)} %reduce-scatter.14.cloned.1.call-done), channel_id=1, replica_groups=mesh['zc'=4,'core'=2,'fsdp'=4] {'zc'}, dimensions={0}, use_global_device_ids=true | all-gather | bytes 983040 | tf_op jit(solution)/shard_map/all_gather | solution.py:140
  819.0 39.0 %psum.7 = f32[4,3072]{1,0:T(4,128)S(1)} all-reduce(f32[4,3072]{1,0:T(4,128)S(1)} %constant_dynamic-update-slice_fusion.7), channel_id=1, replica_groups=mesh['zc'=4,'core'=2,'fsdp'=4] {'zc','core','fsdp'}, use_global_device_ids=true, to_apply=%region_34.35 | all-reduce | flops 12288 | bytes 98304 | tf_op jit(solution)/shard_map/psum | solution.py:340
  860.9 4.1 convert_element_type.314
  865.0 4.2 convert_element_type.316
  (674 shorter events, 254.1 us)
Async XLA Ops:
  7.2 107.9 %copy-start = (bf16[256,4096]{1,0:T(8,128)(2,1)S(1)}, bf16[256,4096]{1,0:T(8,128)(2,1)}, u32[]{:S(2)}) copy-start(bf16[256,4096]{1,0:T(8,128)(2,1)} %param.32) | copy-start | bytes 6291460
  7.2 60.2 %all-gather.13.cloned.1.call-start = ((), (), s32[]{:S(2)}) async-start(), calls=%async_computation.23 | async-start | bytes 9437184 | tf_op jit(solution)/shard_map/all_gather | solution.py:115
  50.7 10.7 %copy-start.13 = (bf16[4,1,2,32,1024]{4,3,2,1,0:T(8,128)(2,1)S(1)}, bf16[4,1,2,32,1024]{4,3,2,1,0:T(8,128)(2,1)}, u32[]{:S(2)}) copy-start(bf16[4,1,2,32,1024]{4,3,2,1,0:T(8,128)(2,1)} %param.20) | copy-start | bytes 1572868
  50.8 190.9 %all-gather.31.cloned.1.call-start = ((), (), s32[]{:S(2)}) async-start(), calls=%async_computation.41 | async-start | bytes 9437184 | tf_op jit(solution)/shard_map/all_gather | solution.py:239
  110.9 17.2 %all-to-all-start.3 = ((bf16[4,128,1024]{2,1,0:T(8,128)(2,1)}), bf16[4,128,1024]{2,1,0:T(8,128)(2,1)}, u32[]{:S(2)}, u32[]{:S(2)}) async-start(bf16[4,128,1024]{2,1,0:T(8,128)(2,1)} %broadcast_in_dim.66), calls=%async_computation.3 | async-start | bytes 2097152 | tf_op jit(solution)/shard_map/all_to_all | solution.py:108
  131.8 51.8 %all-to-all-start.4 = ((bf16[4,128,4096]{2,1,0:T(8,128)(2,1)}), bf16[4,128,4096]{2,1,0:T(8,128)(2,1)}, u32[]{:S(2)}, u32[]{:S(2)}) async-start(bf16[4,128,4096]{2,1,0:T(8,128)(2,1)} %broadcast_in_dim.67), calls=%async_computation.4 | async-start | bytes 8388608 | tf_op jit(solution)/shard_map/all_to_all | solution.py:108
  136.6 166.8 %all-gather.15.cloned.1.call-start = ((), (), s32[]{:S(2)}) async-start(), calls=%async_computation.24 | async-start | bytes 3145728 | tf_op jit(solution)/shard_map/all_gather | solution.py:115
  137.4 169.4 %all-gather.17.cloned.1.call-start = ((), (), s32[]{:S(2)}) async-start(), calls=%async_computation.25 | async-start | bytes 12582912 | tf_op jit(solution)/shard_map/all_gather | solution.py:115
  187.9 51.9 %all-to-all-start.5 = ((bf16[4,512,1024]{2,1,0:T(8,128)(2,1)}), bf16[4,512,1024]{2,1,0:T(8,128)(2,1)}, u32[]{:S(2)}, u32[]{:S(2)}) async-start(bf16[4,512,1024]{2,1,0:T(8,128)(2,1)} %broadcast_in_dim.68), calls=%async_computation.5 | async-start | bytes 8388608 | tf_op jit(solution)/shard_map/all_to_all | solution.py:108
  192.9 123.4 %all-gather.19.cloned.1.call-start = ((), (), s32[]{:S(2)}) async-start(), calls=%async_computation.26 | async-start | bytes 12582912 | tf_op jit(solution)/shard_map/all_gather | solution.py:115
  291.3 10.7 %all-to-all-start.2 = ((bf16[4,2,128,1,256]{4,1,0,3,2:T(2,128)(2,1)}), bf16[4,2,128,1,256]{4,1,0,3,2:T(2,128)(2,1)S(1)}, u32[]{:S(2)}, u32[]{:S(2)}) async-start(bf16[4,2,128,1,256]{4,1,0,3,2:T(2,128)(2,1)} %copy.104), calls=%async_computation.2 | async-start | bytes 1048576 | tf_op jit(solution)/shard_map/all_to_all | solution.py:249
  305.8 26.2 %copy-start.15 = (f32[256,1024]{1,0:T(8,128)}, f32[256,1024]{1,0:T(8,128)S(1)}, u32[]{:S(2)}) copy-start(f32[256,1024]{1,0:T(8,128)S(1)} %get-tuple-element.303) | copy-start | bytes 3145732
  306.8 9.5 %copy-start.19 = (bf16[4,1,2,32,1024]{4,3,2,1,0:T(8,128)(2,1)S(1)}, bf16[4,1,2,32,1024]{4,3,2,1,0:T(8,128)(2,1)}, u32[]{:S(2)}) copy-start(bf16[4,1,2,32,1024]{4,3,2,1,0:T(8,128)(2,1)} %param.21) | copy-start | bytes 1572868
  316.2 12.6 %copy-start.66 = (bf16[4,256,4096]{2,1,0:T(8,128)(2,1)S(1)}, bf16[4,256,4096]{2,1,0:T(8,128)(2,1)}, u32[]{:S(2)}) copy-start(bf16[4,256,4096]{2,1,0:T(8,128)(2,1)} %all-gather.17.cloned.1.call-done) | copy-start | bytes 25165828
  337.1 11.3 %all-to-all-start.6 = ((bf16[4,2,32,4,256]{4,2,1,0,3:T(8,128)(2,1)}), bf16[4,2,32,4,256]{4,2,1,0,3:T(8,128)(2,1)S(1)}, u32[]{:S(2)}, u32[]{:S(2)}) async-start(bf16[4,2,32,4,256]{4,2,1,0,3:T(8,128)(2,1)} %copy.107), calls=%async_computation.6 | async-start | bytes 1048576 | tf_op jit(solution)/shard_map/all_to_all | solution.py:277
  340.6 156.9 %reduce-scatter.20.cloned.1.call-start = ((), (), s32[]{:S(2)}) async-start(), calls=%async_computation.33 | async-start | bytes 12582912 | tf_op jit(solution)/shard_map/reduce_scatter | solution.py:129
  348.4 225.0 %reduce-scatter.10.cloned.1.call-start = ((), (), s32[]{:S(2)}) async-start(), calls=%async_computation.27 | async-start | bytes 9437184 | tf_op jit(solution)/shard_map/reduce_scatter | solution.py:288
  482.4 130.1 %reduce-scatter.24.cloned.1.call-start = ((), (), s32[]{:S(2)}) async-start(), calls=%async_computation.37 | async-start | bytes 12582912 | tf_op jit(solution)/shard_map/reduce_scatter | solution.py:129
  497.4 169.1 %reduce-scatter.22.cloned.1.call-start = ((), (), s32[]{:S(2)}) async-start(), calls=%async_computation.34 | async-start | bytes 1310720 | tf_op jit(solution)/shard_map/reduce_scatter | solution.py:139
  553.5 113.7 %reduce-scatter.16.cloned.1.call-start = ((), (), s32[]{:S(2)}) async-start(), calls=%async_computation.31 | async-start | bytes 3145728 | tf_op jit(solution)/shard_map/reduce_scatter | solution.py:129
  557.9 18.1 %all-to-all-start.7 = ((bf16[4,2,128,1,256]{4,1,0,3,2:T(2,128)(2,1)}), bf16[4,2,128,1,256]{4,1,0,3,2:T(2,128)(2,1)S(1)}, u32[]{:S(2)}, u32[]{:S(2)}) async-start(bf16[4,2,128,1,256]{4,1,0,3,2:T(2,128)(2,1)} %copy.110), calls=%async_computation.7 | async-start | bytes 1048576 | tf_op jit(solution)/shard_map/all_to_all | solution.py:299
  574.7 16.1 %copy-start.45 = (f32[4,2,32]{2,1,0:T(2,128)S(1)}, f32[4,2,32]{2,1,0:T(2,128)}, u32[]{:S(2)}) copy-start(f32[4,2,32]{2,1,0:T(2,128)} %copy-done.44) | copy-start | bytes 3076
  574.7 16.1 %copy-start.14 = (bf16[4,1,2,32,1024]{4,3,2,1,0:T(8,128)(2,1)S(1)}, bf16[4,1,2,32,1024]{4,3,2,1,0:T(8,128)(2,1)}, u32[]{:S(2)}) copy-start(bf16[4,1,2,32,1024]{4,3,2,1,0:T(8,128)(2,1)} %param.20) | copy-start | bytes 1572868
  576.0 10.2 %all-to-all-start.8 = ((bf16[4,2,128,1,256]{4,1,0,3,2:T(2,128)(2,1)}), bf16[4,2,128,1,256]{4,1,0,3,2:T(2,128)(2,1)S(1)}, u32[]{:S(2)}, u32[]{:S(2)}) async-start(bf16[4,2,128,1,256]{4,1,0,3,2:T(2,128)(2,1)} %copy.116), calls=%async_computation.9 | async-start | bytes 1048576 | tf_op jit(solution)/shard_map/all_to_all | solution.py:302
  579.7 12.2 %copy-start.50 = (f32[4,2,32]{2,1,0:T(2,128)S(1)}, f32[4,2,32]{2,1,0:T(2,128)}, u32[]{:S(2)}) copy-start(f32[4,2,32]{2,1,0:T(2,128)} %get-tuple-element.298) | copy-start | bytes 3076
  579.7 12.3 %copy-start.49 = (f32[4,256]{1,0:T(4,128)S(1)}, f32[4,256]{1,0:T(4,128)}, u32[]{:S(2)}) copy-start(f32[4,256]{1,0:T(4,128)} %get-tuple-element.297) | copy-start | bytes 12292
  579.7 12.3 %copy-start.48 = (f32[4,256]{1,0:T(4,128)S(1)}, f32[4,256]{1,0:T(4,128)}, u32[]{:S(2)}) copy-start(f32[4,256]{1,0:T(4,128)} %get-tuple-element.288) | copy-start | bytes 12292
  586.3 10.8 %all-to-all-start.9 = ((bf16[4,2,128,1,256]{4,1,0,3,2:T(2,128)(2,1)}), bf16[4,2,128,1,256]{4,1,0,3,2:T(2,128)(2,1)}, u32[]{:S(2)}, u32[]{:S(2)}) async-start(bf16[4,2,128,1,256]{4,1,0,3,2:T(2,128)(2,1)} %copy.119), calls=%async_computation.10 | async-start | bytes 1048576 | tf_op jit(solution)/shard_map/all_to_all | solution.py:305
  590.4 90.2 %reduce-scatter.12.cloned.1.call-start = ((), (), s32[]{:S(2)}) async-start(), calls=%async_computation.28 | async-start | bytes 9437184 | tf_op jit(solution)/shard_map/reduce_scatter | solution.py:129
  612.5 85.0 %reduce-scatter.26.cloned.1.call-start = ((), (), s32[]{:S(2)}) async-start(), calls=%async_computation.38 | async-start | bytes 1310720 | tf_op jit(solution)/shard_map/reduce_scatter | solution.py:139
  666.4 59.1 %all-gather.23.cloned.1.call-start = ((), (), s32[]{:S(2)}) async-start(), calls=%async_computation.35 | async-start | bytes 1310720 | tf_op jit(solution)/shard_map/all_gather | solution.py:140
  680.6 34.3 %all-to-all-start.10 = ((bf16[4,128,3072]{2,1,0:T(8,128)(2,1)}), bf16[4,128,3072]{2,1,0:T(8,128)(2,1)}, u32[]{:S(2)}, u32[]{:S(2)}) async-start(bf16[4,128,3072]{2,1,0:T(8,128)(2,1)} %bitcast.305), calls=%async_computation.12 | async-start | bytes 6291456 | tf_op jit(solution)/shard_map/all_to_all | solution.py:131
  685.3 69.1 %all-gather.27.cloned.1.call-start = ((), (), s32[]{:S(2)}) async-start(), calls=%async_computation.39 | async-start | bytes 1310720 | tf_op jit(solution)/shard_map/all_gather | solution.py:140
  697.5 78.4 %reduce-scatter.18.cloned.1.call-start = ((), (), s32[]{:S(2)}) async-start(), calls=%async_computation.32 | async-start | bytes 327680 | tf_op jit(solution)/shard_map/reduce_scatter | solution.py:139
  698.5 102.2 %reduce-scatter.14.cloned.1.call-start = ((), (), s32[]{:S(2)}) async-start(), calls=%async_computation.29 | async-start | bytes 983040 | tf_op jit(solution)/shard_map/reduce_scatter | solution.py:139
  718.5 36.2 %copy-start.47 = (f32[1,2,4,128]{3,2,1,0:T(4,128)S(1)}, f32[1,2,4,128]{3,2,1,0:T(4,128)}, u32[]{:S(2)}) copy-start(f32[1,2,4,128]{3,2,1,0:T(4,128)} %get-tuple-element.291) | copy-start | bytes 12292
  718.5 37.4 %copy-start.46 = (f32[1024]{0:T(1024)S(1)}, f32[1024]{0:T(1024)}, u32[]{:S(2)}) copy-start(f32[1024]{0:T(1024)} %get-tuple-element.244) | copy-start | bytes 12292
  718.5 37.4 %copy-start.56 = (f32[1024]{0:T(1024)S(1)}, f32[1024]{0:T(1024)}, u32[]{:S(2)}) copy-start(f32[1024]{0:T(1024)} %get-tuple-element.199) | copy-start | bytes 12292
  718.5 37.5 %copy-start.55 = (f32[1024]{0:T(1024)S(1)}, f32[1024]{0:T(1024)}, u32[]{:S(2)}) copy-start(f32[1024]{0:T(1024)} %get-tuple-element.203) | copy-start | bytes 12292
  718.5 37.5 %copy-start.51 = (f32[4096]{0:T(1024)S(1)}, f32[4096]{0:T(1024)}, u32[]{:S(2)}) copy-start(f32[4096]{0:T(1024)} %get-tuple-element.308) | copy-start | bytes 49156
  718.5 37.5 %copy-start.16 = (f32[256,1024]{1,0:T(8,128)S(1)}, f32[256,1024]{1,0:T(8,128)}, u32[]{:S(2)}) copy-start(f32[256,1024]{1,0:T(8,128)} %copy-done.15) | copy-start | bytes 3145732
  718.5 142.4 %all-gather.25.cloned.1.call-start = ((), (), s32[]{:S(2)}) async-start(), calls=%async_computation.36 | async-start | bytes 3145728 | tf_op jit(solution)/shard_map/all_gather | solution.py:141
  725.6 139.4 %all-gather.29.cloned.1.call-start = ((), (), s32[]{:S(2)}) async-start(), calls=%async_computation.40 | async-start | bytes 3145728 | tf_op jit(solution)/shard_map/all_gather | solution.py:141
  754.4 114.8 %all-gather.21.cloned.1.call-start = ((), (), s32[]{:S(2)}) async-start(), calls=%async_computation.30 | async-start | bytes 2359296 | tf_op jit(solution)/shard_map/all_gather | solution.py:141
  797.3 62.2 %copy-start.18 = (f32[256,1024]{1,0:T(8,128)S(1)}, f32[256,1024]{1,0:T(8,128)}, u32[]{:S(2)}) copy-start(f32[256,1024]{1,0:T(8,128)} %copy-done.17) | copy-start | bytes 3145732
  797.3 62.2 %copy-start.21 = (bf16[4,1,2,32,1024]{4,3,2,1,0:T(8,128)(2,1)S(1)}, bf16[4,1,2,32,1024]{4,3,2,1,0:T(8,128)(2,1)}, u32[]{:S(2)}) copy-start(bf16[4,1,2,32,1024]{4,3,2,1,0:T(8,128)(2,1)} %param.21) | copy-start | bytes 1572868
  797.3 62.2 %copy-start.26 = (f32[256,1024]{1,0:T(8,128)S(1)}, f32[256,1024]{1,0:T(8,128)}, u32[]{:S(2)}) copy-start(f32[256,1024]{1,0:T(8,128)} %get-tuple-element.307) | copy-start | bytes 3145732
  797.3 62.2 %copy-start.53 = (f32[256]{0:T(256)S(1)}, f32[256]{0:T(256)}, u32[]{:S(2)}) copy-start(f32[256]{0:T(256)} %copy-done.52) | copy-start | bytes 3076
  (92 other events, 186.8 us)
Sparse Core Ops, SparseCore 0:
  50.9 16.4 all-gather.12
  109.8 81.4 all-gather.30
  192.9 9.0 all-gather.14
  203.4 21.0 all-gather.16
  239.9 19.8 all-gather.18
  348.5 17.7 reduce-scatter.19
  482.5 90.8 reduce-scatter.9
  575.7 14.8 reduce-scatter.23
  592.9 28.5 reduce-scatter.21
  624.2 8.2 reduce-scatter.15
  634.8 15.3 reduce-scatter.11
  666.5 30.8 reduce-scatter.25
  699.0 26.4 all-gather.22
  727.0 27.3 all-gather.26
  756.5 19.3 reduce-scatter.17
  778.6 22.0 reduce-scatter.13
  802.1 10.1 all-gather.24
  813.6 11.7 all-gather.28
  827.0 10.9 all-gather.20
where the time goes:
time: 889 us; the launch traced here: 880 us
  blocking collectives  263 us (30%)
  waiting for transfers between devices  216 us (24%)
  local copies, waits for them, and re-layouts  150 us (17%)
  matrix products  132 us (15%)
  other arithmetic  63.4 us (7%)
  starting transfers between devices  38.7 us (4%)
  between operations  15.6 us (2%)
    all_to_all x3, blocking collectives, reduce_weight_grad(): lax.all_to_all(grad.reshape((fsdp_size, -1) + grad.shape[1:]), 'fsdp', sp...  115 us
    all_to_all x3, waiting for transfers between devices, gather_weight(): lax.all_to_all(jnp.broadcast_to(piece[None], (fsdp_size,) + piece.shape),...  104 us
    dot_general x52, matrix products, contract_last(): lax.dot_general(left, right, (((1,), (1,)), ((), ())), preferred_element_...  52.5 us
    all_to_all x1, blocking collectives, gather_weight(): lax.all_to_all(jnp.broadcast_to(piece[None], (fsdp_size,) + piece.shape),...  41.7 us
    psum x1, blocking collectives, shards(): packed = lax.psum(packed.astype(jnp.float32), CTX + ('fsdp',))  39 us
    dot_general x36, matrix products, contract_first(): lax.dot_general(left, right, (((0,), (0,)), ((), ())), preferred_element_...  36 us
    all_gather x2, waiting for transfers between devices, reduce_weight_grad(): grad = lax.all_gather(grad, 'zc', axis=0, tiled=True)  35.7 us
    all_gather x2, blocking collectives, reduce_weight_grad(): grad = lax.all_gather(grad, 'zc', axis=0, tiled=True)  33.7 us
  transfers between devices with their start and end apart: 28, of which 14 were waited for; matrix products, arithmetic and copies ran while one was open for 31% of the time, Pallas kernels for 0%

commit v1 on v0

--- a/solution.py
+++ b/solution.py
@@ -337,7 +337,7 @@
         proj_bias_grad,
     )
     packed = jnp.concatenate([grad.reshape(fsdp_size, -1) for grad in vector_grads], axis=1)
-    packed = lax.psum(packed.astype(jnp.float32), CTX + ("fsdp",))
+    packed = jnp.sum(lax.all_gather(packed.astype(jnp.float32), CTX + ("fsdp",)), axis=0)
     packed = lax.dynamic_index_in_dim(packed, lax.axis_index("fsdp"), 0, keepdims=False)
     vector_totals = []
     offset = 0

time: 889 us -> 985 us (1.11)
  waiting for transfers between devices: 216 us -> 395 us
  blocking collectives: 263 us -> 164 us
  starting transfers between devices: 38.7 us -> 48.7 us
    all_to_all x1 -> x3, waiting for transfers between devices: 16.4 us -> 79.5 us  [reduce_weight_grad(): lax.all_to_all(grad.reshape((fsdp_size, -1) + grad.shape[1:]), 'fsdp', sp...]
    all_to_all x3 -> x1, blocking collectives: 115 us -> 53.5 us  [reduce_weight_grad(): lax.all_to_all(grad.reshape((fsdp_size, -1) + grad.shape[1:]), 'fsdp', sp...]
    reduce_scatter x1, waiting for transfers between devices: 12 us -> 61.3 us  [shards(): lax.psum_scatter(kv_grads.reshape(ctx_size * seq_count * pair_len, 2 * gr...]
    psum x1 -> x0, blocking collectives: 39 us -> none  [shards(): packed = lax.psum(packed.astype(jnp.float32), CTX + ('fsdp',))]
    all_gather x0 -> x1, waiting for transfers between devices: none -> 32.2 us  [shards(): lax.all_gather(packed.astype(jnp.float32), CTX + ('fsdp',))]
    all_gather x3, waiting for transfers between devices: 0.01 us -> 25.3 us  [reduce_weight_grad(): grad = lax.all_gather(grad, 'core', axis=0, tiled=True)]
    all_gather x2, waiting for transfers between devices: 35.7 us -> 21.5 us  [reduce_weight_grad(): grad = lax.all_gather(grad, 'zc', axis=0, tiled=True)]
    reduce_scatter x4, waiting for transfers between devices: 26.4 us -> 40.2 us  [reduce_weight_grad(): grad = lax.psum_scatter(grad, 'zc', scatter_dimension=0, tiled=True)]
  transfers between devices with their start and end apart: 28 -> 31, of which waited for: 14 -> 18; matrix products, arithmetic and copies ran while one was open for 31% -> 17% of each run, Pallas kernels for 0% -> 0%
where the time goes in v1:
time: 985 us; the launch traced here: 976 us
  waiting for transfers between devices  395 us (40%)
  blocking collectives  164 us (17%)
  local copies, waits for them, and re-layouts  154 us (16%)
  matrix products  131 us (13%)
  other arithmetic  65.2 us (7%)
  starting transfers between devices  48.7 us (5%)
  between operations  15.6 us (2%)
    all_to_all x3, waiting for transfers between devices, gather_weight(): lax.all_to_all(jnp.broadcast_to(piece[None], (fsdp_size,) + piece.shape),...  104 us
    all_to_all x3, waiting for transfers between devices, reduce_weight_grad(): lax.all_to_all(grad.reshape((fsdp_size, -1) + grad.shape[1:]), 'fsdp', sp...  79.5 us
    reduce_scatter x1, waiting for transfers between devices, shards(): lax.psum_scatter(kv_grads.reshape(ctx_size * seq_count * pair_len, 2 * gr...  61.3 us
    all_to_all x1, blocking collectives, reduce_weight_grad(): lax.all_to_all(grad.reshape((fsdp_size, -1) + grad.shape[1:]), 'fsdp', sp...  53.5 us
    dot_general x52, matrix products, contract_last(): lax.dot_general(left, right, (((1,), (1,)), ((), ())), preferred_element_...  51.9 us
    all_to_all x1, blocking collectives, gather_weight(): lax.all_to_all(jnp.broadcast_to(piece[None], (fsdp_size,) + piece.shape),...  41.7 us
    reduce_scatter x4, waiting for transfers between devices, reduce_weight_grad(): grad = lax.psum_scatter(grad, 'zc', scatter_dimension=0, tiled=True)  40.2 us
    dot_general x36, matrix products, contract_first(): lax.dot_general(left, right, (((0,), (0,)), ((), ())), preferred_element_...  35.9 us
  transfers between devices with their start and end apart: 31, of which 18 were waited for; matrix products, arithmetic and copies ran while one was open for 17% of the time, Pallas kernels for 0%

profile of v1, /device:TPU:0, one launch (start us, length us, event | category | flops | bytes accessed | tf_op | source)
XLA Modules:
  0.0 975.7 jit_solution(10298605169202098431)
XLA Ops:
  9.0 41.7 %all_to_all.124 = bf16[4,128,3072]{2,1,0:T(8,128)(2,1)} all-to-all(bf16[4,128,3072]{2,1,0:T(8,128)(2,1)S(1)} %broadcast_in_dim.65), channel_id=1, replica_groups=mesh['zc'=4,'core'=2,'fsdp'=4] {'fsdp'}, dimensions={0} | all-to-all | bytes 6291456 | tf_op jit(solution)/shard_map/all_to_all | solution.py:108
  53.2 7.6 all-gather
  62.8 4.6 all-gather.16.cloned.1.call-done
  67.4 4.6 fusion.102
  83.4 23.9 %all_to_all.125 = bf16[4,2,32,4,768]{4,2,1,0,3:T(8,128)(2,1)S(1)} all-to-all(bf16[4,2,32,4,768]{4,2,1,0,3:T(8,128)(2,1)S(1)} %pad_maximum_fusion), channel_id=1, replica_groups=mesh['zc'=4,'core'=2,'fsdp'=4] {'fsdp'}, dimensions={3} | all-to-all | bytes 3145728 | tf_op jit(solution)/shard_map/all_to_all | solution.py:230
  110.9 4.3 all-to-all-start.3
  116.2 11.9 %all-to-all-done.3 = bf16[4,128,1024]{2,1,0:T(8,128)(2,1)} async-done(((bf16[4,128,1024]{2,1,0:T(8,128)(2,1)}), bf16[4,128,1024]{2,1,0:T(8,128)(2,1)}, u32[]{:S(2)}, u32[]{:S(2)}) %all-to-all-start.3) | async-done | bytes 1048608 | tf_op jit(solution)/shard_map/all_to_all | solution.py:108
  131.8 4.8 all-to-all-start.4
  137.4 46.1 %all-to-all-done.4 = bf16[4,128,4096]{2,1,0:T(8,128)(2,1)} async-done(((bf16[4,128,4096]{2,1,0:T(8,128)(2,1)}), bf16[4,128,4096]{2,1,0:T(8,128)(2,1)}, u32[]{:S(2)}, u32[]{:S(2)}) %all-to-all-start.4) | async-done | bytes 4194336 | tf_op jit(solution)/shard_map/all_to_all | solution.py:108
  187.9 5.0 all-to-all-start.5
  193.7 46.1 %all-to-all-done.5 = bf16[4,512,1024]{2,1,0:T(8,128)(2,1)} async-done(((bf16[4,512,1024]{2,1,0:T(8,128)(2,1)}), bf16[4,512,1024]{2,1,0:T(8,128)(2,1)}, u32[]{:S(2)}, u32[]{:S(2)}) %all-to-all-start.5) | async-done | bytes 4194336 | tf_op jit(solution)/shard_map/all_to_all | solution.py:108
  241.7 6.5 fusion.98
  248.2 41.8 %while.26 = (s32[]{:T(128)}, bf16[4,256,256]{2,1,0:T(8,128)(2,1)S(1)}, f32[4,256,4]{1,2,0:T(4,128)}, s32[4,2048]{1,0:T(4,128)S(1)}, s32[4,256]{1,0:T(4,128)S(1)}...) while((s32[]{:T(128)}, ...), condition=%wide.region_11.12_spmd, body=%wide.region_2.11_spmd.sunk | while | flops 554240000 | bytes 35092604 | solution.py:246
  295.5 6.8 all-to-all-done.2
  306.7 9.5 multiply_convert_fusion.4
  316.3 12.1 %convert_reduce_fusion = (f32[4096]{0:T(1024)}, bf16[256,4096]{1,0:T(8,128)(2,1)S(1)}) fusion(f32[256,4096]{1,0:T(8,128)} %get-tuple-element.305, bf16[4096,1024]{1,0:T(8,128)(2,1)} %bitcast.375, bf16[256,1024]{1,0:T(8,128)(2,1)S(1)} %bitcast.286), kind=kOutput, calls=%fused_computation.141 | convolution fusion | flops 2170548224 | bytes 15220736 | tf_op jit(solution)/shard_map/dot_general | solution.py:27
  340.4 6.3 all-to-all-done.6
  347.5 117.9 %while.27 = (s32[]{:T(128)}, bf16[4,256,256]{2,1,0:T(8,128)(2,1)}, bf16[4,2048,256]{2,1,0:T(8,128)(2,1)}, bf16[4,2048,256]{2,1,0:T(8,128)(2,1)}, s32[4,2048]{1,0...) while((s32[]{:T(128)}, bf16[4,256,256]{2,1,0:T(8,128)(2,1)}, ...), condition=%wide.region_21.22_spmd, body=%wide.region_16.21_spmd.sunk | while | flops 1370029056 | bytes 166414960 | solution.py:280
  465.4 7.5 maximum_bitcast_fusion.5
  473.0 7.6 copy.115
  482.5 5.9 convolution_convert_fusion.9
  492.7 4.8 copy.126
  497.5 5.6 convolution_convert_fusion.8
  509.0 61.3 %reduce-scatter.10.cloned.1.call-done = bf16[1024,512]{1,0:T(8,128)(2,1)} async-done(((bf16[8192,512]{1,0:T(8,128)(2,1)}), bf16[1024,512]{1,0:T(8,128)(2,1)}) %reduce-scatter.10.cloned.1.call-update) | async-done | bytes 1048592 | tf_op jit(solution)/shard_map/reduce_scatter | solution.py:288
  576.5 10.9 %reduce-scatter.20.cloned.1.call-done = bf16[512,4096]{1,0:T(8,128)(2,1)} async-done(((bf16[1024,4096]{1,0:T(8,128)(2,1)}), bf16[512,4096]{1,0:T(8,128)(2,1)}) %reduce-scatter.20.cloned.1.call-update) | async-done | bytes 4194320 | tf_op jit(solution)/shard_map/reduce_scatter | solution.py:129
  587.4 4.9 all-to-all-start.12
  593.6 46.8 %all-to-all-done.12 = bf16[4,128,4096]{2,1,0:T(8,128)(2,1)} async-done(((bf16[4,128,4096]{2,1,0:T(8,128)(2,1)}), bf16[4,128,4096]{2,1,0:T(8,128)(2,1)}, u32[]{:S(2)}, u32[]{:S(2)}) %all-to-all-start.12) | async-done | bytes 4194336 | tf_op jit(solution)/shard_map/all_to_all | solution.py:131
  640.4 4.2 all-to-all-start.9
  646.8 4.2 reduce_sum.334
  654.6 5.7 fusion.90
  663.5 4.5 convolution_convert_fusion.10
  668.1 53.5 %all_to_all.126 = bf16[4,512,1024]{2,1,0:T(8,128)(2,1)} all-to-all(bf16[4,512,1024]{2,1,0:T(8,128)(2,1)} %bitcast.301), channel_id=1, replica_groups=mesh['zc'=4,'core'=2,'fsdp'=4] {'fsdp'}, dimensions={0} | all-to-all | bytes 8388608 | tf_op jit(solution)/shard_map/all_to_all | solution.py:131
  721.6 4.4 reduce_sum.335
  733.2 4.7 all-to-all-start.10
  738.0 15.0 %reduce-scatter.26.cloned.1.call-done = bf16[128,1024]{1,0:T(8,128)(2,1)} async-done(((bf16[512,1024]{1,0:T(8,128)(2,1)}), bf16[128,1024]{1,0:T(8,128)(2,1)}) %reduce-scatter.26.cloned.1.call-update) | async-done | bytes 262160 | tf_op jit(solution)/shard_map/reduce_scatter | solution.py:139
  753.0 19.8 %all-to-all-done.10 = bf16[4,128,3072]{2,1,0:T(8,128)(2,1)} async-done(((bf16[4,128,3072]{2,1,0:T(8,128)(2,1)}), bf16[4,128,3072]{2,1,0:T(8,128)(2,1)}, u32[]{:S(2)}, u32[]{:S(2)}) %all-to-all-start.10) | async-done | bytes 3145760 | tf_op jit(solution)/shard_map/all_to_all | solution.py:131
  776.5 4.3 all-to-all-start.11
  781.1 12.9 %all-to-all-done.11 = bf16[4,128,1024]{2,1,0:T(8,128)(2,1)} async-done(((bf16[4,128,1024]{2,1,0:T(8,128)(2,1)}), bf16[4,128,1024]{2,1,0:T(8,128)(2,1)}, u32[]{:S(2)}, u32[]{:S(2)}) %all-to-all-start.11) | async-done | bytes 1048608 | tf_op jit(solution)/shard_map/all_to_all | solution.py:131
  802.1 21.5 %all-gather.30.cloned.1.call-done = bf16[512,1024]{1,0:T(8,128)(2,1)} async-done(((bf16[128,1024]{1,0:T(8,128)(2,1)}), bf16[512,1024]{1,0:T(8,128)(2,1)}) %all-gather.30.cloned.1.call-update) | async-done | bytes 1048592 | tf_op jit(solution)/shard_map/all_gather | solution.py:140
  823.7 25.2 %reduce-scatter.14.cloned.1.call-done = bf16[32,3072]{1,0:T(8,128)(2,1)} async-done(((bf16[128,3072]{1,0:T(8,128)(2,1)}), bf16[32,3072]{1,0:T(8,128)(2,1)}) %reduce-scatter.14.cloned.1.call-update) | async-done | bytes 196624 | tf_op jit(solution)/shard_map/reduce_scatter | solution.py:139
  848.9 20.7 %all_gather.60 = bf16[128,3072]{1,0:T(8,128)(2,1)} all-gather(bf16[32,3072]{1,0:T(8,128)(2,1)} %reduce-scatter.14.cloned.1.call-done), channel_id=1, replica_groups=mesh['zc'=4,'core'=2,'fsdp'=4] {'zc'}, dimensions={0}, use_global_device_ids=true | all-gather | bytes 983040 | tf_op jit(solution)/shard_map/all_gather | solution.py:140
  869.6 7.2 fusion.78
  876.8 14.8 %all_gather.62 = bf16[128,1024]{1,0:T(8,128)(2,1)S(1)} all-gather(bf16[32,1024]{1,0:T(8,128)(2,1)} %reduce-scatter.18.cloned.1.call-done), channel_id=1, replica_groups=mesh['zc'=4,'core'=2,'fsdp'=4] {'zc'}, dimensions={0}, use_global_device_ids=true | all-gather | bytes 327680 | tf_op jit(solution)/shard_map/all_gather | solution.py:140
  896.4 32.2 %all-gather.36.cloned.1.call-done = f32[32,4,3072]{2,1,0:T(4,128)} async-done(((f32[1,4,3072]{2,1,0:T(4,128)}), f32[32,4,3072]{2,1,0:T(4,128)}) %all-gather.36.cloned.1.call-update) | async-done | bytes 1572880 | tf_op jit(solution)/shard_map/all_gather | solution.py:340
  931.6 7.9 all-gather.28.cloned.1.call-done
  943.6 9.2 all-gather.32.cloned.1.call-done
  952.8 4.2 convert_element_type.316
  957.1 8.2 all-gather.24.cloned.1.call-done
  (679 shorter events, 277.2 us)
Async XLA Ops:
  7.2 107.9 %copy-start = (bf16[256,4096]{1,0:T(8,128)(2,1)S(1)}, bf16[256,4096]{1,0:T(8,128)(2,1)}, u32[]{:S(2)}) copy-start(bf16[256,4096]{1,0:T(8,128)(2,1)} %param.32) | copy-start | bytes 6291460
  7.2 60.2 %all-gather.16.cloned.1.call-start = ((), (), s32[]{:S(2)}) async-start(), calls=%async_computation.23 | async-start | bytes 9437184 | tf_op jit(solution)/shard_map/all_gather | solution.py:115
  50.7 10.8 %copy-start.13 = (bf16[4,1,2,32,1024]{4,3,2,1,0:T(8,128)(2,1)S(1)}, bf16[4,1,2,32,1024]{4,3,2,1,0:T(8,128)(2,1)}, u32[]{:S(2)}) copy-start(bf16[4,1,2,32,1024]{4,3,2,1,0:T(8,128)(2,1)} %param.20) | copy-start | bytes 1572868
  50.8 190.9 %all-gather.34.cloned.1.call-start = ((), (), s32[]{:S(2)}) async-start(), calls=%async_computation.41 | async-start | bytes 9437184 | tf_op jit(solution)/shard_map/all_gather | solution.py:239
  110.9 17.2 %all-to-all-start.3 = ((bf16[4,128,1024]{2,1,0:T(8,128)(2,1)}), bf16[4,128,1024]{2,1,0:T(8,128)(2,1)}, u32[]{:S(2)}, u32[]{:S(2)}) async-start(bf16[4,128,1024]{2,1,0:T(8,128)(2,1)} %broadcast_in_dim.66), calls=%async_computation.3 | async-start | bytes 2097152 | tf_op jit(solution)/shard_map/all_to_all | solution.py:108
  131.8 51.8 %all-to-all-start.4 = ((bf16[4,128,4096]{2,1,0:T(8,128)(2,1)}), bf16[4,128,4096]{2,1,0:T(8,128)(2,1)}, u32[]{:S(2)}, u32[]{:S(2)}) async-start(bf16[4,128,4096]{2,1,0:T(8,128)(2,1)} %broadcast_in_dim.67), calls=%async_computation.4 | async-start | bytes 8388608 | tf_op jit(solution)/shard_map/all_to_all | solution.py:108
  136.7 167.1 %all-gather.18.cloned.1.call-start = ((), (), s32[]{:S(2)}) async-start(), calls=%async_computation.24 | async-start | bytes 3145728 | tf_op jit(solution)/shard_map/all_gather | solution.py:115
  137.4 169.3 %all-gather.20.cloned.1.call-start = ((), (), s32[]{:S(2)}) async-start(), calls=%async_computation.25 | async-start | bytes 12582912 | tf_op jit(solution)/shard_map/all_gather | solution.py:115
  187.9 51.9 %all-to-all-start.5 = ((bf16[4,512,1024]{2,1,0:T(8,128)(2,1)}), bf16[4,512,1024]{2,1,0:T(8,128)(2,1)}, u32[]{:S(2)}, u32[]{:S(2)}) async-start(bf16[4,512,1024]{2,1,0:T(8,128)(2,1)} %broadcast_in_dim.68), calls=%async_computation.5 | async-start | bytes 8388608 | tf_op jit(solution)/shard_map/all_to_all | solution.py:108
  192.9 123.4 %all-gather.22.cloned.1.call-start = ((), (), s32[]{:S(2)}) async-start(), calls=%async_computation.26 | async-start | bytes 12582912 | tf_op jit(solution)/shard_map/all_gather | solution.py:115
  291.4 10.9 %all-to-all-start.2 = ((bf16[4,2,128,1,256]{4,1,0,3,2:T(2,128)(2,1)}), bf16[4,2,128,1,256]{4,1,0,3,2:T(2,128)(2,1)S(1)}, u32[]{:S(2)}, u32[]{:S(2)}) async-start(bf16[4,2,128,1,256]{4,1,0,3,2:T(2,128)(2,1)} %copy.104), calls=%async_computation.2 | async-start | bytes 1048576 | tf_op jit(solution)/shard_map/all_to_all | solution.py:249
  306.1 25.4 %copy-start.15 = (f32[256,1024]{1,0:T(8,128)}, f32[256,1024]{1,0:T(8,128)S(1)}, u32[]{:S(2)}) copy-start(f32[256,1024]{1,0:T(8,128)S(1)} %get-tuple-element.303) | copy-start | bytes 3145732
  306.7 9.6 copy-start.30
  306.7 9.6 copy-start.19
  316.3 12.1 %copy-start.66 = (bf16[4,256,4096]{2,1,0:T(8,128)(2,1)S(1)}, bf16[4,256,4096]{2,1,0:T(8,128)(2,1)}, u32[]{:S(2)}) copy-start(bf16[4,256,4096]{2,1,0:T(8,128)(2,1)} %all-gather.20.cloned.1.call-done) | copy-start | bytes 25165828
  336.6 10.0 %all-to-all-start.6 = ((bf16[4,2,32,4,256]{4,2,1,0,3:T(8,128)(2,1)}), bf16[4,2,32,4,256]{4,2,1,0,3:T(8,128)(2,1)S(1)}, u32[]{:S(2)}, u32[]{:S(2)}) async-start(bf16[4,2,32,4,256]{4,2,1,0,3:T(8,128)(2,1)} %copy.107), calls=%async_computation.6 | async-start | bytes 1048576 | tf_op jit(solution)/shard_map/all_to_all | solution.py:277
  340.1 230.1 %reduce-scatter.10.cloned.1.call-start = ((), (), s32[]{:S(2)}) async-start(), calls=%async_computation.27 | async-start | bytes 9437184 | tf_op jit(solution)/shard_map/reduce_scatter | solution.py:288
  480.6 106.8 %reduce-scatter.20.cloned.1.call-start = ((), (), s32[]{:S(2)}) async-start(), calls=%async_computation.33 | async-start | bytes 12582912 | tf_op jit(solution)/shard_map/reduce_scatter | solution.py:129
  488.4 179.7 %reduce-scatter.24.cloned.1.call-start = ((), (), s32[]{:S(2)}) async-start(), calls=%async_computation.37 | async-start | bytes 12582912 | tf_op jit(solution)/shard_map/reduce_scatter | solution.py:129
  505.5 67.3 %all-to-all-start.7 = ((bf16[4,2,128,1,256]{4,1,0,3,2:T(2,128)(2,1)}), bf16[4,2,128,1,256]{4,1,0,3,2:T(2,128)(2,1)S(1)}, u32[]{:S(2)}, u32[]{:S(2)}) async-start(bf16[4,2,128,1,256]{4,1,0,3,2:T(2,128)(2,1)} %copy.110), calls=%async_computation.7 | async-start | bytes 1048576 | tf_op jit(solution)/shard_map/all_to_all | solution.py:299
  572.8 14.5 %all-to-all-start.8 = ((bf16[4,2,128,1,256]{4,1,0,3,2:T(2,128)(2,1)}), bf16[4,2,128,1,256]{4,1,0,3,2:T(2,128)(2,1)S(1)}, u32[]{:S(2)}, u32[]{:S(2)}) async-start(bf16[4,2,128,1,256]{4,1,0,3,2:T(2,128)(2,1)} %copy.116), calls=%async_computation.9 | async-start | bytes 1048576 | tf_op jit(solution)/shard_map/all_to_all | solution.py:302
  587.4 53.1 %all-to-all-start.12 = ((bf16[4,128,4096]{2,1,0:T(8,128)(2,1)}), bf16[4,128,4096]{2,1,0:T(8,128)(2,1)}, u32[]{:S(2)}, u32[]{:S(2)}) async-start(bf16[4,128,4096]{2,1,0:T(8,128)(2,1)} %bitcast.302), calls=%async_computation.18 | async-start | bytes 8388608 | tf_op jit(solution)/shard_map/all_to_all | solution.py:131
  592.2 52.4 %copy-start.44 = (f32[4,2,32]{2,1,0:T(2,128)S(1)}, f32[4,2,32]{2,1,0:T(2,128)}, u32[]{:S(2)}) copy-start(f32[4,2,32]{2,1,0:T(2,128)} %copy-done.43) | copy-start | bytes 3076
  592.3 52.5 %copy-start.14 = (bf16[4,1,2,32,1024]{4,3,2,1,0:T(8,128)(2,1)S(1)}, bf16[4,1,2,32,1024]{4,3,2,1,0:T(8,128)(2,1)}, u32[]{:S(2)}) copy-start(bf16[4,1,2,32,1024]{4,3,2,1,0:T(8,128)(2,1)} %param.20) | copy-start | bytes 1572868
  592.3 54.4 %copy-start.50 = (f32[4,2,32]{2,1,0:T(2,128)S(1)}, f32[4,2,32]{2,1,0:T(2,128)}, u32[]{:S(2)}) copy-start(f32[4,2,32]{2,1,0:T(2,128)} %get-tuple-element.298) | copy-start | bytes 3076
  592.3 54.5 %copy-start.49 = (f32[4,256]{1,0:T(4,128)S(1)}, f32[4,256]{1,0:T(4,128)}, u32[]{:S(2)}) copy-start(f32[4,256]{1,0:T(4,128)} %get-tuple-element.297) | copy-start | bytes 12292
  592.3 54.5 %copy-start.48 = (f32[4,256]{1,0:T(4,128)S(1)}, f32[4,256]{1,0:T(4,128)}, u32[]{:S(2)}) copy-start(f32[4,256]{1,0:T(4,128)} %get-tuple-element.288) | copy-start | bytes 12292
  640.4 12.4 %all-to-all-start.9 = ((bf16[4,2,128,1,256]{4,1,0,3,2:T(2,128)(2,1)}), bf16[4,2,128,1,256]{4,1,0,3,2:T(2,128)(2,1)}, u32[]{:S(2)}, u32[]{:S(2)}) async-start(bf16[4,2,128,1,256]{4,1,0,3,2:T(2,128)(2,1)} %copy.119), calls=%async_computation.10 | async-start | bytes 1048576 | tf_op jit(solution)/shard_map/all_to_all | solution.py:305
  644.6 87.9 %reduce-scatter.22.cloned.1.call-start = ((), (), s32[]{:S(2)}) async-start(), calls=%async_computation.34 | async-start | bytes 1310720 | tf_op jit(solution)/shard_map/reduce_scatter | solution.py:139
  651.0 82.2 %reduce-scatter.12.cloned.1.call-start = ((), (), s32[]{:S(2)}) async-start(), calls=%async_computation.28 | async-start | bytes 9437184 | tf_op jit(solution)/shard_map/reduce_scatter | solution.py:129
  668.0 84.9 %reduce-scatter.26.cloned.1.call-start = ((), (), s32[]{:S(2)}) async-start(), calls=%async_computation.38 | async-start | bytes 1310720 | tf_op jit(solution)/shard_map/reduce_scatter | solution.py:139
  726.0 50.5 %reduce-scatter.16.cloned.1.call-start = ((), (), s32[]{:S(2)}) async-start(), calls=%async_computation.31 | async-start | bytes 3145728 | tf_op jit(solution)/shard_map/reduce_scatter | solution.py:129
  732.5 68.9 %all-gather.26.cloned.1.call-start = ((), (), s32[]{:S(2)}) async-start(), calls=%async_computation.35 | async-start | bytes 1310720 | tf_op jit(solution)/shard_map/all_gather | solution.py:140
  733.2 39.6 %all-to-all-start.10 = ((bf16[4,128,3072]{2,1,0:T(8,128)(2,1)}), bf16[4,128,3072]{2,1,0:T(8,128)(2,1)}, u32[]{:S(2)}, u32[]{:S(2)}) async-start(bf16[4,128,3072]{2,1,0:T(8,128)(2,1)} %bitcast.306), calls=%async_computation.12 | async-start | bytes 6291456 | tf_op jit(solution)/shard_map/all_to_all | solution.py:131
  737.9 85.7 %all-gather.30.cloned.1.call-start = ((), (), s32[]{:S(2)}) async-start(), calls=%async_computation.39 | async-start | bytes 1310720 | tf_op jit(solution)/shard_map/all_gather | solution.py:140
  753.0 95.9 %reduce-scatter.14.cloned.1.call-start = ((), (), s32[]{:S(2)}) async-start(), calls=%async_computation.29 | async-start | bytes 983040 | tf_op jit(solution)/shard_map/reduce_scatter | solution.py:139
  776.5 17.4 %all-to-all-start.11 = ((bf16[4,128,1024]{2,1,0:T(8,128)(2,1)}), bf16[4,128,1024]{2,1,0:T(8,128)(2,1)}, u32[]{:S(2)}, u32[]{:S(2)}) async-start(bf16[4,128,1024]{2,1,0:T(8,128)(2,1)} %bitcast.330), calls=%async_computation.15 | async-start | bytes 2097152 | tf_op jit(solution)/shard_map/all_to_all | solution.py:131
  780.8 96.0 %reduce-scatter.18.cloned.1.call-start = ((), (), s32[]{:S(2)}) async-start(), calls=%async_computation.32 | async-start | bytes 327680 | tf_op jit(solution)/shard_map/reduce_scatter | solution.py:139
  796.2 132.4 %all-gather.36.cloned.1.call-start = ((), (), s32[]{:S(2)}) async-start(), calls=%async_computation.42 | async-start | bytes 1622016 | tf_op jit(solution)/shard_map/all_gather | solution.py:340
  798.9 24.8 %copy-start.47 = (f32[1,2,4,128]{3,2,1,0:T(4,128)S(1)}, f32[1,2,4,128]{3,2,1,0:T(4,128)}, u32[]{:S(2)}) copy-start(f32[1,2,4,128]{3,2,1,0:T(4,128)} %get-tuple-element.291) | copy-start | bytes 12292
  800.5 69.1 %copy-start.16 = (f32[256,1024]{1,0:T(8,128)S(1)}, f32[256,1024]{1,0:T(8,128)}, u32[]{:S(2)}) copy-start(f32[256,1024]{1,0:T(8,128)} %copy-done.15) | copy-start | bytes 3145732
  801.3 138.2 %all-gather.28.cloned.1.call-start = ((), (), s32[]{:S(2)}) async-start(), calls=%async_computation.36 | async-start | bytes 3145728 | tf_op jit(solution)/shard_map/all_gather | solution.py:141
  801.9 150.9 %all-gather.32.cloned.1.call-start = ((), (), s32[]{:S(2)}) async-start(), calls=%async_computation.40 | async-start | bytes 3145728 | tf_op jit(solution)/shard_map/all_gather | solution.py:141
  823.6 141.6 %all-gather.24.cloned.1.call-start = ((), (), s32[]{:S(2)}) async-start(), calls=%async_computation.30 | async-start | bytes 2359296 | tf_op jit(solution)/shard_map/all_gather | solution.py:141
  876.8 18.1 %copy-start.18 = (f32[256,1024]{1,0:T(8,128)S(1)}, f32[256,1024]{1,0:T(8,128)}, u32[]{:S(2)}) copy-start(f32[256,1024]{1,0:T(8,128)} %copy-done.17) | copy-start | bytes 3145732
  876.8 18.1 %copy-start.53 = (f32[256]{0:T(256)S(1)}, f32[256]{0:T(256)}, u32[]{:S(2)}) copy-start(f32[256]{0:T(256)} %copy-done.52) | copy-start | bytes 3076
  876.8 18.1 %copy-start.25 = (f32[256,1024]{1,0:T(8,128)S(1)}, f32[256,1024]{1,0:T(8,128)}, u32[]{:S(2)}) copy-start(f32[256,1024]{1,0:T(8,128)} %get-tuple-element.307) | copy-start | bytes 3145732
  952.8 15.8 %copy-start.1 = (bf16[256,4096]{1,0:T(8,128)(2,1)S(1)}, bf16[256,4096]{1,0:T(8,128)(2,1)}, u32[]{:S(2)}) copy-start(bf16[256,4096]{1,0:T(8,128)(2,1)} %param.32) | copy-start | bytes 6291460
  (95 other events, 195.8 us)
Sparse Core Ops, SparseCore 0:
  50.9 16.4 all-gather.15
  109.8 81.4 all-gather.33
  192.9 9.0 all-gather.17
  203.4 21.0 all-gather.19
  239.9 19.8 all-gather.21
  480.7 89.5 reduce-scatter.9
  572.5 14.8 reduce-scatter.19
  589.7 17.6 reduce-scatter.23
  651.2 28.8 reduce-scatter.21
  682.2 12.5 reduce-scatter.11
  726.2 26.7 reduce-scatter.25
  755.6 8.2 reduce-scatter.15
  765.5 29.2 all-gather.25
  796.2 27.3 all-gather.29
  826.3 22.5 reduce-scatter.13
  851.0 20.8 reduce-scatter.17
  875.3 53.2 all-gather.35
  930.0 9.4 all-gather.27
  941.0 11.7 all-gather.31
  954.2 10.9 all-gather.23
